TPU v7x, 512 devices: a whole 4x8x8 slice. The times are simulated.
512 devices in a mesh: section: 8 (over y), expert: 32 (over z, x_hi, core), dp: 2 (over x_lo).
Axes of the slice: x: 4 (x_hi: 2, x_lo: 2; x = x_hi * 2 + x_lo), y: 8, z: 8, core: 2. Of those that a mesh axis runs over, the one named last changes fastest.
Arguments:
- blocks: bfloat16 [8, 512, 7168], P('section', ('expert', 'dp')), may hold values from -6 to 6
- gains: float32 [8, 7168], P('section'), may hold values from 0.1 to 1.9
- w_gate: bfloat16 [8, 7168, 4096], P('section', 'dp', 'expert'), may hold values from -0.0625 to 0.0625
- w_up: bfloat16 [8, 7168, 4096], P('section', 'dp', 'expert'), may hold values from -0.0625 to 0.0625
- w_down: bfloat16 [8, 7168, 4096], P('section', 'dp', 'expert'), may hold values from -0.1875 to 0.1875
- expert_ids: int32 [8, 2, 512, 2], P('section', None, ('expert', 'dp')), may hold values from 0 to 3, all different within a row; in each aligned block of 8 rows (0 to 7, 8 to 15, ..., all dimensions but the last counted through in order) at most 5 rows name the same one
- combine: float32 [8, 2, 512, 2], P('section', None, ('expert', 'dp')), may hold values from 0.2 to 1
Outputs:
- finished: bfloat16 [8, 512, 7168], P('section', ('expert', 'dp'))
Inputs may be any that keep to these rules, and one draw needn't show every extreme that they name: `expert_ids`: each token names 2 different experts; within the 8 tokens of one device (aligned blocks), no expert is named more than 5 times, a bound that some block reaches.
All inputs are finite; a program needn't handle non-finite values.
Results may differ from a plain program's by a relative error of at most 0.0073.
Values may be sent and summed in bfloat16 or wider, within the bound.
No kernel may reach another device: no remote copies, remote signals or barrier semaphores. Data moves between devices by JAX's collectives and lax.ppermute only.
A program may use at most 64 MiB of HBM per device.

v0:
```python
from functools import partial
import jax
import jax.numpy as jnp
from jax import lax
from jax.sharding import PartitionSpec as P


def passed_along(array, axis, by):
    length = lax.axis_size(axis)
    return lax.ppermute(array, axis, [(i, (i + by) % length) for i in range(length)])


def expert_rows(arrived, gate_full, up_full, down_full):
    sources, slot_count, model_width = arrived.shape
    flat_rows = arrived.reshape(sources * slot_count, model_width)
    gate_act = jnp.dot(flat_rows, gate_full, preferred_element_type=jnp.float32)
    upward = jnp.dot(flat_rows, up_full, preferred_element_type=jnp.float32)
    hidden = (jax.nn.silu(gate_act) * upward).astype(jnp.bfloat16)
    output = lax.dot_general(
        hidden, down_full, (((1,), (1,)), ((), ())), preferred_element_type=jnp.float32
    )
    output = output.astype(jnp.bfloat16).reshape(sources, slot_count, model_width)
    return lax.all_to_all(output, "expert", split_axis=0, concat_axis=0, tiled=True)


def moe_layer(stream, gain_row, weights, routes, mixing):
    owners = lax.axis_size("expert")
    experts = max(2, owners // 8)
    span = owners // experts
    tok_rows, model_width = stream.shape
    fan_out = routes.shape[1]
    capacity = min(tok_rows, max(2, 5 * tok_rows * fan_out // (4 * experts)))
    widened = stream.astype(jnp.float32)
    inv_rms = lax.rsqrt(jnp.mean(widened * widened, axis=1, keepdims=True) + 1e-06)
    normed = (widened * inv_rms * gain_row[None, :]).astype(jnp.bfloat16)
    flat_ids = routes.reshape(-1)
    count_all = flat_ids.shape[0]
    chosen = (flat_ids[:, None] == jnp.arange(experts, dtype=jnp.int32)[None, :]).astype(
        jnp.float32
    )
    triangle = (jnp.arange(count_all)[:, None] >= jnp.arange(count_all)[None, :]).astype(
        jnp.float32
    )
    running = jnp.dot(triangle, chosen, preferred_element_type=jnp.float32)
    slot_of = jnp.sum(chosen * (running - 1.0), axis=1).astype(jnp.int32)
    target = flat_ids * capacity + slot_of
    placing = jnp.arange(experts * capacity, dtype=jnp.int32)[:, None] == target[None, :]
    placing = (
        placing.reshape(experts * capacity, tok_rows, fan_out).any(axis=2).astype(jnp.bfloat16)
    )
    outgoing = jnp.dot(placing, normed, preferred_element_type=jnp.float32).astype(jnp.bfloat16)
    outgoing = jnp.repeat(outgoing.reshape(experts, capacity, model_width), span, axis=0)
    gate_full, up_full, down_full = weights
    worker = partial(expert_rows, gate_full=gate_full, up_full=up_full, down_full=down_full)
    returned = worker(lax.all_to_all(outgoing, "expert", split_axis=0, concat_axis=0, tiled=True))
    summed = jnp.sum(
        returned.reshape(experts, span, capacity, model_width).astype(jnp.float32), axis=1
    )
    expert_out = summed.astype(jnp.bfloat16).reshape(experts * capacity, model_width)
    picked = jnp.take(expert_out, target, axis=0)
    picked = picked.reshape(tok_rows, fan_out, model_width)
    mixed_sum = jnp.sum(mixing[:, :, None] * picked.astype(jnp.float32), axis=1)
    return (widened + mixed_sum).astype(jnp.bfloat16)


def on_device(blocks, gains, w_gate, w_up, w_down, expert_ids, combine):
    stream = blocks[0]
    turns = expert_ids.shape[1]
    weights = None
    for layer_turn in range(turns):
        if layer_turn > 0:
            stream = passed_along(stream, "section", 1)
        weights = (
            lax.all_gather(w_gate[0], "dp", axis=0, tiled=True),
            lax.all_gather(w_up[0], "dp", axis=0, tiled=True),
            lax.all_gather(w_down[0], "dp", axis=0, tiled=True),
        )
        stream = moe_layer(
            stream, gains[0], weights, expert_ids[0, layer_turn], combine[0, layer_turn]
        )
    return stream[None]


def solution(mesh):
    in_specs = (
        P("section", ("expert", "dp"), None),
        P("section", None),
        P("section", "dp", "expert"),
        P("section", "dp", "expert"),
        P("section", "dp", "expert"),
        P("section", None, ("expert", "dp"), None),
        P("section", None, ("expert", "dp"), None),
    )
    out_specs = P("section", ("expert", "dp"), None)
    return jax.shard_map(
        on_device, mesh=mesh, in_specs=in_specs, out_specs=out_specs, check_vma=False
    )
```

profile of v0, /device:TPU:32, one launch (start us, length us, event | category | flops | bytes accessed | tf_op | source)
XLA Modules:
  0.0 485.9 jit_solution(11815583365687878870)
XLA Ops:
  6.5 0.7 all-gather.7.cloned.1.call-update
  7.3 0.7 fusion.64
  8.0 0.1 copy.25
  8.0 0.1 eq.59
  8.1 0.1 fusion.28
  8.3 0.1 convert_element_type.84
  8.4 0.1 copy.26
  8.4 0.1 copy.28
  8.5 0.1 eq.66
  8.6 0.1 fusion.29
  8.8 0.1 convert_element_type.94
  8.8 0.1 copy.29
  8.9 0.7 bitcast_add_fusion.1
  9.6 0.1 fusion.58
  9.7 1.1 fusion.34
  10.8 1.2 convolution_convert_fusion.3
  12.0 0.1 reshape.113
  12.1 2.3 broadcast_in_dim.15
  14.4 13.3 %all-to-all-start = ((bf16[32,5,7168]{2,1,0:T(8,128)(2,1)}), bf16[32,5,7168]{2,1,0:T(8,128)(2,1)}, u32[]{:S(2)}, u32[]{:S(2)}) async-start(bf16[32,5,7168]{2,1,0:T(8,128)(2,1)} %bitcast.62), calls=%async_computation | async-start | bytes 7340032 | tf_op jit(solution)/shard_map/all_to_all | solution.py:55
  27.7 0.0 all-gather.11.cloned.1.call-start
  27.7 0.7 all-gather.11.cloned.1.call-update
  28.4 0.0 all-gather.9.cloned.1.call-start
  28.5 0.7 all-gather.9.cloned.1.call-update
  29.2 83.9 %all-to-all-done = bf16[32,5,7168]{2,1,0:T(8,128)(2,1)} async-done(((bf16[32,5,7168]{2,1,0:T(8,128)(2,1)}), bf16[32,5,7168]{2,1,0:T(8,128)(2,1)}, u32[]{:S(2)}, u32[]{:S(2)}) %all-to-all-start) | async-done | bytes 2293792 | tf_op jit(solution)/shard_map/all_to_all | solution.py:55
  113.1 3.3 reshape.115
  116.4 0.0 all-gather.7.cloned.1.call-done
  116.4 2.2 fusion.8
  118.7 0.0 all-gather.11.cloned.1.call-done
  118.7 41.1 %all-gather.9.cloned.1.call-done = bf16[1,7168,128]{2,1,0:T(8,128)(2,1)} async-done(((bf16[1,3584,128]{2,1,0:T(8,128)(2,1)}), bf16[1,7168,128]{2,1,0:T(8,128)(2,1)}) %all-gather.9.cloned.1.call-update) | async-done | bytes 1835024 | tf_op jit(solution)/shard_map/all_gather | solution.py:75
  159.8 4.9 %convolution_convert_fusion.1 = bf16[160,7168]{1,0:T(8,128)(2,1)} fusion(bf16[1,7168,128]{2,1,0:T(8,128)(2,1)} %all-gather.11.cloned.1.call-done, bf16[160,7168]{1,0:T(8,128)(2,1)S(1)} %reshape.115, bf16[1,7168,128]{2,1,0:T(8,128)(2,1)} %all-gather.9.cloned.1.call-done, f32[160,128]{1,0:T(8,128)S(1)} %fusion.8), kind=kOutput, calls=%fused_computation.3 | convolution fusion | flops 588472320 | bytes 8339456 | tf_op jit(solution)/shard_map/dot_general | solution.py:19
  164.6 4.6 reshape.116
  169.2 10.1 %all-to-all-start.1 = ((bf16[32,5,7168]{2,1,0:T(8,128)(2,1)}), bf16[32,5,7168]{2,1,0:T(8,128)(2,1)}, u32[]{:S(2)}, u32[]{:S(2)}) async-start(bf16[32,5,7168]{2,1,0:T(8,128)(2,1)} %reshape.116), calls=%async_computation.1 | async-start | bytes 7340032 | tf_op jit(solution)/shard_map/all_to_all | solution.py:23
  179.4 0.1 copy.24
  179.5 85.3 %all-to-all-done.1 = bf16[32,5,7168]{2,1,0:T(8,128)(2,1)} async-done(((bf16[32,5,7168]{2,1,0:T(8,128)(2,1)}), bf16[32,5,7168]{2,1,0:T(8,128)(2,1)}, u32[]{:S(2)}, u32[]{:S(2)}) %all-to-all-start.1) | async-done | bytes 2293792 | tf_op jit(solution)/shard_map/all_to_all | solution.py:23
  264.8 2.8 bitcast_reduce_fusion.1
  267.6 0.1 reshape.118
  267.7 0.0 copy-start
  267.7 0.0 copy-start.1
  267.7 0.7 gather_fusion
  268.4 0.1 select_convert_fusion.1
  268.5 0.3 reshape.126
  268.8 0.6 multiply_reduce_fusion.1
  269.5 2.5 collective-permute-start
  272.0 0.1 fusion.59
  272.1 5.3 %collective-permute-done = bf16[8,7168]{1,0:T(8,128)(2,1)S(1)} collective-permute-done((bf16[8,7168]{1,0:T(8,128)(2,1)S(1)}, bf16[8,7168]{1,0:T(8,128)(2,1)S(1)}, u32[]{:S(2)}, u32[]{:S(2)}) %collective-permute-start) | collective-permute-done | bytes 114720 | tf_op jit(solution)/shard_map/ppermute | solution.py:10
  277.4 0.2 fusion.30
  277.6 0.3 convolution_convert_fusion.2
  277.9 0.1 reshape.119
  278.0 0.4 broadcast_in_dim.16
  278.4 90.5 %all_to_all.20 = bf16[32,5,7168]{2,1,0:T(8,128)(2,1)} all-to-all(bf16[32,5,7168]{2,1,0:T(8,128)(2,1)S(1)} %bitcast.63), channel_id=1, replica_groups=mesh['section'=8,'expert'=32,'dp'=2] {'expert'}, dimensions={0} | all-to-all | bytes 4587520 | tf_op jit(solution)/shard_map/all_to_all | solution.py:55
  368.9 3.3 reshape.121
  372.2 2.2 fusion.6
  374.4 4.9 %convolution_convert_fusion = bf16[160,7168]{1,0:T(8,128)(2,1)} fusion(bf16[1,7168,128]{2,1,0:T(8,128)(2,1)} %all-gather.11.cloned.1.call-done, bf16[160,7168]{1,0:T(8,128)(2,1)S(1)} %reshape.121, bf16[1,7168,128]{2,1,0:T(8,128)(2,1)} %all-gather.9.cloned.1.call-done, f32[160,128]{1,0:T(8,128)S(1)} %fusion.6), kind=kOutput, calls=%fused_computation.2 | convolution fusion | flops 588472320 | bytes 8339456 | tf_op jit(solution)/shard_map/dot_general | solution.py:19
  379.3 4.6 reshape.122
  383.9 4.8 all-to-all-start.3
  388.7 0.1 copy.27
  388.8 85.3 %all-to-all-done.3 = bf16[32,5,7168]{2,1,0:T(8,128)(2,1)} async-done(((bf16[32,5,7168]{2,1,0:T(8,128)(2,1)}), bf16[32,5,7168]{2,1,0:T(8,128)(2,1)}, u32[]{:S(2)}, u32[]{:S(2)}) %all-to-all-start.3) | async-done | bytes 2293792 | tf_op jit(solution)/shard_map/all_to_all | solution.py:23
  474.1 2.8 bitcast_reduce_fusion
  476.9 0.1 reshape.124
  477.0 0.7 gather_fusion.1
  477.7 0.1 select_convert_fusion
  477.8 0.3 reshape.127
  478.1 0.6 multiply_reduce_fusion
  478.7 0.7 fusion.39
  (15 shorter events, 0.1 us)
Async XLA Ops:
  6.5 109.9 %all-gather.7.cloned.1.call-start = ((), (), s32[]{:S(2)}) async-start(), calls=%async_computation.4 | async-start | bytes 2752512 | tf_op jit(solution)/shard_map/all_gather | solution.py:74
  14.4 98.7 %all-to-all-start = ((bf16[32,5,7168]{2,1,0:T(8,128)(2,1)}), bf16[32,5,7168]{2,1,0:T(8,128)(2,1)}, u32[]{:S(2)}, u32[]{:S(2)}) async-start(bf16[32,5,7168]{2,1,0:T(8,128)(2,1)} %bitcast.62), calls=%async_computation | async-start | bytes 7340032 | tf_op jit(solution)/shard_map/all_to_all | solution.py:55
  27.7 91.0 %all-gather.11.cloned.1.call-start = ((), (), s32[]{:S(2)}) async-start(), calls=%async_computation.6 | async-start | bytes 2752512 | tf_op jit(solution)/shard_map/all_gather | solution.py:76
  28.4 131.3 %all-gather.9.cloned.1.call-start = ((), (), s32[]{:S(2)}) async-start(), calls=%async_computation.5 | async-start | bytes 2752512 | tf_op jit(solution)/shard_map/all_gather | solution.py:75
  169.2 10.1 %copy-start.2 = (f32[1,2,8,2]{2,3,1,0:T(2,128)S(1)}, f32[1,2,8,2]{2,3,1,0:T(2,128)}, u32[]{:S(2)}) copy-start(f32[1,2,8,2]{2,3,1,0:T(2,128)} %param.15) | copy-start | bytes 388
  169.2 95.6 %all-to-all-start.1 = ((bf16[32,5,7168]{2,1,0:T(8,128)(2,1)}), bf16[32,5,7168]{2,1,0:T(8,128)(2,1)}, u32[]{:S(2)}, u32[]{:S(2)}) async-start(bf16[32,5,7168]{2,1,0:T(8,128)(2,1)} %reshape.116), calls=%async_computation.1 | async-start | bytes 7340032 | tf_op jit(solution)/shard_map/all_to_all | solution.py:23
  267.7 1.7 copy-start
  267.7 9.9 %copy-start.1 = (f32[1,7168]{1,0:T(1,128)S(1)}, f32[1,7168]{1,0:T(1,128)}, u32[]{:S(2)}) copy-start(f32[1,7168]{1,0:T(1,128)} %param.10) | copy-start | bytes 86020
  269.5 7.9 %collective-permute-start = (bf16[8,7168]{1,0:T(8,128)(2,1)S(1)}, bf16[8,7168]{1,0:T(8,128)(2,1)S(1)}, u32[]{:S(2)}, u32[]{:S(2)}) collective-permute-start(bf16[8,7168]{1,0:T(8,128)(2,1)S(1)} %fusion.37), channel_id=1, source_target_pairs={{0,64},{64,128},{128,192},{192,256},{256,320},{320,384},{384,448},... | collective-permute-start | bytes 344072 | tf_op jit(solution)/shard_map/ppermute | solution.py:10
  383.9 90.2 %all-to-all-start.3 = ((bf16[32,5,7168]{2,1,0:T(8,128)(2,1)}), bf16[32,5,7168]{2,1,0:T(8,128)(2,1)}, u32[]{:S(2)}, u32[]{:S(2)}) async-start(bf16[32,5,7168]{2,1,0:T(8,128)(2,1)} %reshape.122), calls=%async_computation.3 | async-start | bytes 7340032 | tf_op jit(solution)/shard_map/all_to_all | solution.py:23
Sparse Core Ops, SparseCore 0:
  9.4 63.5 all-gather.6
  75.1 42.5 all-gather.10
  119.8 39.9 all-gather.8
where the time goes:
time: 487 us; the launch traced here: 486 us
  waiting for transfers between devices  303 us (62%)
  blocking collectives  90.5 us (19%)
  starting transfers between devices  30.8 us (6%)
  local copies, waits for them, and re-layouts  22.2 us (5%)
  matrix products  16 us (3%)
  between operations  13.4 us (3%)
  other arithmetic  9.93 us (2%)
    all_to_all x2, waiting for transfers between devices, expert_rows(): lax.all_to_all(output, 'expert', split_axis=0, concat_axis=0, tiled=True)  171 us
    all_to_all x1, blocking collectives, moe_layer(): lax.all_to_all(outgoing, 'expert', split_axis=0, concat_axis=0, tiled=True)  90.5 us
    all_to_all x1, waiting for transfers between devices, moe_layer(): lax.all_to_all(outgoing, 'expert', split_axis=0, concat_axis=0, tiled=True)  83.9 us
    all_gather x1, waiting for transfers between devices, on_device(): lax.all_gather(w_up[0], 'dp', axis=0, tiled=True)  41.1 us
    all_to_all x2, starting transfers between devices, expert_rows(): lax.all_to_all(output, 'expert', split_axis=0, concat_axis=0, tiled=True)  15 us
    all_to_all x1, starting transfers between devices, moe_layer(): lax.all_to_all(outgoing, 'expert', split_axis=0, concat_axis=0, tiled=True)  13.3 us
    dot_general x2, matrix products, expert_rows(): lax.dot_general(hidden, down_full, (((1,), (1,)), ((), ())), preferred_el...  9.76 us
  transfers between devices with their start and end apart: 7, of which 5 were waited for; matrix products, arithmetic and copies ran while one was open for 3% of the time, Pallas kernels for 0%

commit v1 on v0

--- a/solution.py
+++ b/solution.py
@@ -72,7 +72,9 @@
             stream = passed_along(stream, "section", 1)
         weights = (
             lax.all_gather(w_gate[0], "dp", axis=0, tiled=True),
-            lax.all_gather(w_up[0], "dp", axis=0, tiled=True),
+            jnp.concatenate(
+                lax.all_to_all(jnp.stack([w_up[0]] * lax.axis_size("dp")), "dp", 0, 0), axis=0
+            ),
             lax.all_gather(w_down[0], "dp", axis=0, tiled=True),
         )
         stream = moe_layer(

time: 487 us -> 472 us (0.969)
  waiting for transfers between devices: 303 us -> 281 us
    all_gather x1 -> x0, waiting for transfers between devices: 41.1 us -> none  [on_device(): lax.all_gather(w_up[0], 'dp', axis=0, tiled=True)]
    all_to_all x0 -> x1, waiting for transfers between devices: none -> 21.7 us  [on_device(): lax.all_to_all(jnp.stack([w_up[0]] * lax.axis_size('dp')), 'dp', 0, 0)]
  transfers between devices with their start and end apart: 7 -> 7, of which waited for: 5 -> 5; matrix products, arithmetic and copies ran while one was open for 3% -> 2% of each run, Pallas kernels for 0% -> 0%
where the time goes in v1:
time: 472 us; the launch traced here: 471 us
  waiting for transfers between devices  281 us (60%)
  blocking collectives  90.5 us (19%)
  starting transfers between devices  35.5 us (8%)
  local copies, waits for them, and re-layouts  22.2 us (5%)
  matrix products  16.1 us (3%)
  between operations  13.7 us (3%)
  other arithmetic  11.4 us (2%)
    all_to_all x2, waiting for transfers between devices, expert_rows(): lax.all_to_all(output, 'expert', split_axis=0, concat_axis=0, tiled=True)  171 us
    all_to_all x1, blocking collectives, moe_layer(): lax.all_to_all(outgoing, 'expert', split_axis=0, concat_axis=0, tiled=True)  90.5 us
    all_to_all x1, waiting for transfers between devices, moe_layer(): lax.all_to_all(outgoing, 'expert', split_axis=0, concat_axis=0, tiled=True)  82.5 us
    all_to_all x1, waiting for transfers between devices, on_device(): lax.all_to_all(jnp.stack([w_up[0]] * lax.axis_size('dp')), 'dp', 0, 0)  21.7 us
    all_to_all x2, starting transfers between devices, expert_rows(): lax.all_to_all(output, 'expert', split_axis=0, concat_axis=0, tiled=True)  15 us
    all_to_all x1, starting transfers between devices, moe_layer(): lax.all_to_all(outgoing, 'expert', split_axis=0, concat_axis=0, tiled=True)  13.3 us
    dot_general x2, matrix products, expert_rows(): lax.dot_general(hidden, down_full, (((1,), (1,)), ((), ())), preferred_el...  9.76 us
  transfers between devices with their start and end apart: 7, of which 5 were waited for; matrix products, arithmetic and copies ran while one was open for 2% of the time, Pallas kernels for 0%

profile of v1, /device:TPU:32, one launch (start us, length us, event | category | flops | bytes accessed | tf_op | source)
XLA Modules:
  0.0 470.8 jit_solution(12169627539251073792)
XLA Ops:
  6.5 0.7 fusion.46
  7.2 0.1 copy.25
  7.3 0.1 eq.59
  7.4 0.1 fusion.10
  7.5 0.1 convert_element_type.84
  7.6 0.1 copy.26
  7.7 0.1 copy.28
  7.8 0.1 eq.66
  7.9 0.1 fusion.11
  8.0 0.1 convert_element_type.94
  8.1 0.1 copy.29
  8.2 0.7 bitcast_add_fusion.1
  8.9 0.1 fusion.40
  9.0 1.1 fusion.16
  10.1 1.2 convolution_convert_fusion.3
  11.3 0.1 reshape.117
  11.4 2.3 broadcast_in_dim.15
  13.7 13.3 %all-to-all-start = ((bf16[32,5,7168]{2,1,0:T(8,128)(2,1)}), bf16[32,5,7168]{2,1,0:T(8,128)(2,1)}, u32[]{:S(2)}, u32[]{:S(2)}) async-start(bf16[32,5,7168]{2,1,0:T(8,128)(2,1)} %bitcast.48), calls=%async_computation | async-start | bytes 7340032 | tf_op jit(solution)/shard_map/all_to_all | solution.py:55
  27.0 0.0 copy-start.1
  27.0 0.0 all-gather.5.cloned.1.call-start
  27.0 0.7 all-gather.5.cloned.1.call-update
  27.7 0.0 all-gather.7.cloned.1.call-start
  27.8 0.7 all-gather.7.cloned.1.call-update
  28.5 1.4 pad_maximum_fusion
  29.9 82.5 %all-to-all-done = bf16[32,5,7168]{2,1,0:T(8,128)(2,1)} async-done(((bf16[32,5,7168]{2,1,0:T(8,128)(2,1)}), bf16[32,5,7168]{2,1,0:T(8,128)(2,1)}, u32[]{:S(2)}, u32[]{:S(2)}) %all-to-all-start) | async-done | bytes 2293792 | tf_op jit(solution)/shard_map/all_to_all | solution.py:55
  112.4 4.7 %all-to-all-start.1 = ((bf16[2,3584,128]{2,1,0:T(8,128)(2,1)}), bf16[2,3584,128]{2,1,0:T(8,128)(2,1)}, u32[]{:S(2)}, u32[]{:S(2)}) async-start(bf16[2,3584,128]{2,1,0:T(8,128)(2,1)} %pad_maximum_fusion), calls=%async_computation.1 | async-start | bytes 3670016 | tf_op jit(solution)/shard_map/all_to_all | solution.py:76
  117.1 3.3 reshape.119
  120.4 0.0 all-gather.5.cloned.1.call-done
  120.4 2.2 fusion.4
  122.7 21.7 %all-to-all-done.1 = bf16[2,3584,128]{2,1,0:T(8,128)(2,1)} async-done(((bf16[2,3584,128]{2,1,0:T(8,128)(2,1)}), bf16[2,3584,128]{2,1,0:T(8,128)(2,1)}, u32[]{:S(2)}, u32[]{:S(2)}) %all-to-all-start.1) | async-done | bytes 1835040 | tf_op jit(solution)/shard_map/all_to_all | solution.py:76
  144.3 4.9 %convolution_convert_fusion.1 = bf16[160,7168]{1,0:T(8,128)(2,1)} fusion(bf16[1,7168,128]{2,1,0:T(8,128)(2,1)} %all-gather.7.cloned.1.call-done, bf16[160,7168]{1,0:T(8,128)(2,1)S(1)} %reshape.119, bf16[7168,128]{1,0:T(8,128)(2,1)} %bitcast.7, f32[160,128]{1,0:T(8,128)S(1)} %fusion.4), kind=kOutput, calls=%fused_computation.3 | convolution fusion | flops 588472320 | bytes 8339456 | tf_op jit(solution)/shard_map/dot_general | solution.py:19
  149.2 4.6 reshape.121
  153.8 10.1 %all-to-all-start.2 = ((bf16[32,5,7168]{2,1,0:T(8,128)(2,1)}), bf16[32,5,7168]{2,1,0:T(8,128)(2,1)}, u32[]{:S(2)}, u32[]{:S(2)}) async-start(bf16[32,5,7168]{2,1,0:T(8,128)(2,1)} %reshape.121), calls=%async_computation.2 | async-start | bytes 7340032 | tf_op jit(solution)/shard_map/all_to_all | solution.py:23
  163.9 0.1 copy.24
  164.0 85.3 %all-to-all-done.2 = bf16[32,5,7168]{2,1,0:T(8,128)(2,1)} async-done(((bf16[32,5,7168]{2,1,0:T(8,128)(2,1)}), bf16[32,5,7168]{2,1,0:T(8,128)(2,1)}, u32[]{:S(2)}, u32[]{:S(2)}) %all-to-all-start.2) | async-done | bytes 2293792 | tf_op jit(solution)/shard_map/all_to_all | solution.py:23
  249.3 2.8 bitcast_reduce_fusion.1
  252.1 0.1 reshape.123
  252.3 0.0 copy-start
  252.3 0.7 gather_fusion
  253.0 0.1 select_convert_fusion.1
  253.1 0.3 reshape.131
  253.4 0.6 multiply_reduce_fusion.1
  254.1 2.5 collective-permute-start
  256.6 0.1 fusion.41
  256.6 5.3 %collective-permute-done = bf16[8,7168]{1,0:T(8,128)(2,1)S(1)} collective-permute-done((bf16[8,7168]{1,0:T(8,128)(2,1)S(1)}, bf16[8,7168]{1,0:T(8,128)(2,1)S(1)}, u32[]{:S(2)}, u32[]{:S(2)}) %collective-permute-start) | collective-permute-done | bytes 114720 | tf_op jit(solution)/shard_map/ppermute | solution.py:10
  262.0 0.2 fusion.12
  262.1 0.3 convolution_convert_fusion.2
  262.5 0.1 reshape.124
  262.6 0.4 broadcast_in_dim.16
  263.0 90.5 %all_to_all.26 = bf16[32,5,7168]{2,1,0:T(8,128)(2,1)} all-to-all(bf16[32,5,7168]{2,1,0:T(8,128)(2,1)S(1)} %bitcast.49), channel_id=1, replica_groups=mesh['section'=8,'expert'=32,'dp'=2] {'expert'}, dimensions={0} | all-to-all | bytes 4587520 | tf_op jit(solution)/shard_map/all_to_all | solution.py:55
  353.5 3.3 reshape.126
  356.7 2.2 fusion.2
  359.0 4.9 %convolution_convert_fusion = bf16[160,7168]{1,0:T(8,128)(2,1)} fusion(bf16[1,7168,128]{2,1,0:T(8,128)(2,1)} %all-gather.7.cloned.1.call-done, bf16[160,7168]{1,0:T(8,128)(2,1)S(1)} %reshape.126, bf16[7168,128]{1,0:T(8,128)(2,1)} %bitcast.7, f32[160,128]{1,0:T(8,128)S(1)} %fusion.2), kind=kOutput, calls=%fused_computation.2 | convolution fusion | flops 588472320 | bytes 8339456 | tf_op jit(solution)/shard_map/dot_general | solution.py:19
  363.9 4.6 reshape.127
  368.4 4.8 %all-to-all-start.4 = ((bf16[32,5,7168]{2,1,0:T(8,128)(2,1)}), bf16[32,5,7168]{2,1,0:T(8,128)(2,1)}, u32[]{:S(2)}, u32[]{:S(2)}) async-start(bf16[32,5,7168]{2,1,0:T(8,128)(2,1)} %reshape.127), calls=%async_computation.4 | async-start | bytes 7340032 | tf_op jit(solution)/shard_map/all_to_all | solution.py:23
  373.3 0.1 copy.27
  373.4 85.3 %all-to-all-done.4 = bf16[32,5,7168]{2,1,0:T(8,128)(2,1)} async-done(((bf16[32,5,7168]{2,1,0:T(8,128)(2,1)}), bf16[32,5,7168]{2,1,0:T(8,128)(2,1)}, u32[]{:S(2)}, u32[]{:S(2)}) %all-to-all-start.4) | async-done | bytes 2293792 | tf_op jit(solution)/shard_map/all_to_all | solution.py:23
  458.7 2.8 bitcast_reduce_fusion
  461.4 0.1 reshape.129
  461.6 0.7 gather_fusion.1
  462.3 0.1 select_convert_fusion
  462.4 0.3 reshape.132
  462.7 0.6 multiply_reduce_fusion
  463.3 0.7 fusion.21
  (17 shorter events, 0.1 us)
Async XLA Ops:
  13.7 98.7 %all-to-all-start = ((bf16[32,5,7168]{2,1,0:T(8,128)(2,1)}), bf16[32,5,7168]{2,1,0:T(8,128)(2,1)}, u32[]{:S(2)}, u32[]{:S(2)}) async-start(bf16[32,5,7168]{2,1,0:T(8,128)(2,1)} %bitcast.48), calls=%async_computation | async-start | bytes 7340032 | tf_op jit(solution)/shard_map/all_to_all | solution.py:55
  27.0 1.5 copy-start.1
  27.0 93.4 %all-gather.5.cloned.1.call-start = ((), (), s32[]{:S(2)}) async-start(), calls=%async_computation.5 | async-start | bytes 2752512 | tf_op jit(solution)/shard_map/all_gather | solution.py:74
  27.7 116.6 %all-gather.7.cloned.1.call-start = ((), (), s32[]{:S(2)}) async-start(), calls=%async_computation.6 | async-start | bytes 2752512 | tf_op jit(solution)/shard_map/all_gather | solution.py:78
  112.4 31.9 %all-to-all-start.1 = ((bf16[2,3584,128]{2,1,0:T(8,128)(2,1)}), bf16[2,3584,128]{2,1,0:T(8,128)(2,1)}, u32[]{:S(2)}, u32[]{:S(2)}) async-start(bf16[2,3584,128]{2,1,0:T(8,128)(2,1)} %pad_maximum_fusion), calls=%async_computation.1 | async-start | bytes 3670016 | tf_op jit(solution)/shard_map/all_to_all | solution.py:76
  153.8 10.2 %copy-start.3 = (f32[1,2,8,2]{2,3,1,0:T(2,128)S(1)}, f32[1,2,8,2]{2,3,1,0:T(2,128)}, u32[]{:S(2)}) copy-start(f32[1,2,8,2]{2,3,1,0:T(2,128)} %param.15) | copy-start | bytes 388
  153.8 95.6 %all-to-all-start.2 = ((bf16[32,5,7168]{2,1,0:T(8,128)(2,1)}), bf16[32,5,7168]{2,1,0:T(8,128)(2,1)}, u32[]{:S(2)}, u32[]{:S(2)}) async-start(bf16[32,5,7168]{2,1,0:T(8,128)(2,1)} %reshape.121), calls=%async_computation.2 | async-start | bytes 7340032 | tf_op jit(solution)/shard_map/all_to_all | solution.py:23
  252.3 1.7 copy-start
  252.3 9.9 %copy-start.2 = (f32[1,7168]{1,0:T(1,128)S(1)}, f32[1,7168]{1,0:T(1,128)}, u32[]{:S(2)}) copy-start(f32[1,7168]{1,0:T(1,128)} %param.10) | copy-start | bytes 86020
  254.1 7.9 %collective-permute-start = (bf16[8,7168]{1,0:T(8,128)(2,1)S(1)}, bf16[8,7168]{1,0:T(8,128)(2,1)S(1)}, u32[]{:S(2)}, u32[]{:S(2)}) collective-permute-start(bf16[8,7168]{1,0:T(8,128)(2,1)S(1)} %fusion.19), channel_id=1, source_target_pairs={{0,64},{64,128},{128,192},{192,256},{256,320},{320,384},{384,448},... | collective-permute-start | bytes 344072 | tf_op jit(solution)/shard_map/ppermute | solution.py:10
  368.4 90.2 %all-to-all-start.4 = ((bf16[32,5,7168]{2,1,0:T(8,128)(2,1)}), bf16[32,5,7168]{2,1,0:T(8,128)(2,1)}, u32[]{:S(2)}, u32[]{:S(2)}) async-start(bf16[32,5,7168]{2,1,0:T(8,128)(2,1)} %reshape.127), calls=%async_computation.4 | async-start | bytes 7340032 | tf_op jit(solution)/shard_map/all_to_all | solution.py:23
Sparse Core Ops, SparseCore 0:
  29.9 49.2 all-gather.4
  81.3 49.4 all-gather.6
